TPU v7x, 32 devices: a whole 2x2x4 slice. The times are simulated.
32 devices in a mesh: group: 4 (over y, x), dom: 8 (over z, core).
Axes of the slice: x: 2, y: 2, z: 4, core: 2. Of those that a mesh axis runs over, the one named last changes fastest.
Arguments:
- pin_feats: bfloat16 [32768, 256], P(('group', 'dom')), may hold values from -6 to 6
- w_self: bfloat16 [256, 256], replicated, may hold values from -0.375 to 0.375
- w_edge: bfloat16 [4, 256, 256], replicated, may hold values from -0.375 to 0.375
- w_head: bfloat16 [256, 1024], replicated, may hold values from -0.375 to 0.375
- w_out: bfloat16 [1024], replicated, may hold values from -0.1875 to 0.1875
- send_rows: int32 [32, 512], P(('group', 'dom')), may hold values from 0 to 1023
- edge_src: int32 [32, 4, 1024], P(('group', 'dom')), may hold values from 0 to 1535
- edge_dst: int32 [32, 4, 1024], P(('group', 'dom')), may hold values from 0 to 1023
- pin_owner: int32 [32768, 1], P(('group', 'dom')), may hold values from 0 to 31; in each aligned block of 1024 rows (0 to 1023, 1024 to 2047, ...) at most 64 rows name the same one
- pin_net: int32 [32768], P(('group', 'dom')), may hold values from 0 to 255
- net_target: float32 [8192], P(('group', 'dom')), may hold values from -6 to 6
Outputs:
- prediction: float32 [8192], P(('group', 'dom'))
- grad_feats: bfloat16 [32768, 256], P(('group', 'dom'))
- grad_self: float32 [256, 256], replicated
- grad_edge: float32 [4, 256, 256], replicated
- grad_head: float32 [256, 1024], replicated
- grad_out: float32 [1024], replicated
Inputs may be any that keep to these rules, and one draw needn't show every extreme that they name: `pin_owner`: among the pins of one device at most 64 name one owner, and in every draw some device sends exactly 64 pins to some owner.
All inputs are finite; a program needn't handle non-finite values.
Results may differ from a plain program's by a relative error of at most 0.0094.
Values may be sent and summed in bfloat16 or wider, within the bound.
No kernel may reach another device: no remote copies, remote signals or barrier semaphores. Data moves between devices by JAX's collectives and lax.ppermute only.
A program may use at most 64 MiB of HBM per device.

v0:
```python
import math
import jax
import jax.numpy as jnp
from jax import lax
from jax.sharding import PartitionSpec as P

F32 = jnp.float32
BF16 = jnp.bfloat16


def extended(block, sides, width):
    for axis, dim in sides:
        count = lax.axis_size(axis)
        forward = [(i, i + 1) for i in range(count - 1)]
        backward = [(target, source) for source, target in forward]
        low = lax.ppermute(
            lax.slice_in_dim(block, block.shape[dim] - width, None, axis=dim), axis, forward
        )
        high = lax.ppermute(lax.slice_in_dim(block, 0, width, axis=dim), axis, backward)
        block = jnp.concatenate([low, block, high], axis=dim)
    return block


def silu_slope(values):
    sigma_val = jax.nn.sigmoid(values)
    return sigma_val * (1.0 + values * (1.0 - sigma_val))


def one_hot(index, count):
    return (index[..., None] == jnp.arange(count, dtype=index.dtype)).astype(BF16)


def split_dot(spec, left, right):
    return jnp.einsum(
        spec, left, right.astype(F32), precision=lax.Precision.HIGHEST, preferred_element_type=F32
    )


def on_device(
    pin_feats,
    w_self,
    w_edge,
    w_head,
    w_out,
    send_rows,
    edge_src,
    edge_dst,
    pin_owner,
    pin_net,
    net_target,
):
    pin_count, feat_width = pin_feats.shape
    send_list = send_rows[0]
    halo_span = send_list.shape[0] // 2
    send_hot = one_hot(send_list, pin_count)
    outgoing = jnp.dot(send_hot, pin_feats, preferred_element_type=F32).astype(BF16)
    padded = extended(outgoing, (("dom", 0),), halo_span)
    node_table = jnp.concatenate([pin_feats, padded[:halo_span], padded[3 * halo_span :]], 0)
    table_rows = node_table.shape[0]
    sources = edge_src[0]
    endpoints = edge_dst[0]
    src_hot = one_hot(sources, table_rows)
    dst_hot = one_hot(endpoints, pin_count)
    gathered = jnp.einsum("ter,rd->ted", src_hot, node_table, preferred_element_type=F32).astype(
        BF16
    )
    edge_in = jnp.einsum("tep,ted->tpd", dst_hot, gathered, preferred_element_type=F32)
    summed = split_dot("tpk,tkd->pd", edge_in, w_edge)
    degree = jnp.sum(dst_hot.astype(F32), axis=(0, 1))
    inverse = 1.0 / (1.0 + degree)
    preact = jnp.dot(pin_feats, w_self, preferred_element_type=F32) + summed * inverse[:, None]
    hidden = jax.nn.silu(preact).astype(BF16)
    groups = lax.axis_size("group")
    domains = lax.axis_size("dom")
    owners = groups * domains
    capacity = max(2, 2 * pin_count // owners)
    net_count = net_target.shape[0]
    owner_ids = pin_owner[:, 0]
    owner_hot = one_hot(owner_ids, owners)
    earlier = (
        jnp.arange(pin_count, dtype=jnp.int32)[None, :]
        < jnp.arange(pin_count, dtype=jnp.int32)[:, None]
    ).astype(BF16)
    before = jnp.dot(earlier, owner_hot, preferred_element_type=F32)
    slot_rank = jnp.sum(before * owner_hot.astype(F32), axis=1).astype(jnp.int32)
    pin_slot = owner_ids * capacity + slot_rank
    slot_hot = one_hot(pin_slot, owners * capacity)
    net_code = (pin_net + 1).astype(BF16)[:, None]
    slot_nets = (
        jnp.dot(slot_hot.T, net_code, preferred_element_type=F32)[:, 0].astype(jnp.int32) - 1
    )
    slot_nets_in = lax.all_to_all(
        slot_nets.reshape(owners, capacity),
        ("group", "dom"),
        split_axis=0,
        concat_axis=0,
        tiled=True,
    ).reshape(-1)
    outbound = jnp.dot(slot_hot.T, hidden, preferred_element_type=F32).astype(BF16)
    inbound = lax.all_to_all(
        outbound.reshape(owners, capacity, feat_width),
        ("group", "dom"),
        split_axis=0,
        concat_axis=0,
        tiled=True,
    ).reshape(-1, feat_width)
    net_hot = one_hot(slot_nets_in, net_count)
    pooled = jnp.einsum("sn,sd->nd", net_hot, inbound, preferred_element_type=F32)
    pooled_b = pooled.astype(BF16)
    head_pre = jnp.dot(pooled_b, w_head, preferred_element_type=F32)
    activated = jax.nn.silu(head_pre).astype(BF16)
    predicted = jnp.dot(activated, w_out, preferred_element_type=F32)
    misfit = predicted - net_target
    head_grad = (misfit[:, None] * w_out.astype(F32)[None, :] * silu_slope(head_pre)).astype(BF16)
    head_sum = jnp.einsum("nd,nh->dh", pooled_b, head_grad, preferred_element_type=F32)
    out_sum = jnp.dot(misfit, activated.astype(F32), precision=lax.Precision.HIGHEST)
    head_totals = lax.psum(jnp.concatenate([head_sum, out_sum[None, :]], 0), ("group", "dom"))
    net_grad = jnp.einsum("nh,dh->nd", head_grad, w_head, preferred_element_type=F32).astype(BF16)
    returned = jnp.dot(net_hot, net_grad, preferred_element_type=F32).astype(BF16)
    arrived = lax.all_to_all(
        returned.reshape(owners, capacity, feat_width),
        ("group", "dom"),
        split_axis=0,
        concat_axis=0,
        tiled=True,
    ).reshape(-1, feat_width)
    pin_grad = jnp.dot(slot_hot, arrived, preferred_element_type=F32)
    preact_grad = (pin_grad * silu_slope(preact)).astype(BF16)
    self_sum = jnp.einsum("pk,pd->kd", pin_feats, preact_grad, preferred_element_type=F32)
    agg_grad = (preact_grad.astype(F32) * inverse[:, None]).astype(BF16)
    edge_rows = jnp.einsum("tep,pd->ted", dst_hot, agg_grad, preferred_element_type=F32).astype(
        BF16
    )
    edge_sum = jnp.einsum("tek,ted->tkd", gathered, edge_rows, preferred_element_type=F32)
    row_in = jnp.einsum("ter,ted->trd", src_hot, edge_rows, preferred_element_type=F32)
    table_grad = split_dot("trd,tkd->rk", row_in, w_edge)
    local_grad = (
        jnp.einsum("pd,kd->pk", preact_grad, w_self, preferred_element_type=F32)
        + table_grad[:pin_count]
    )
    halo_grad = table_grad[pin_count:].astype(BF16)
    back_padded = extended(halo_grad, (("dom", 0),), halo_span)
    received = jnp.concatenate([back_padded[:halo_span], back_padded[3 * halo_span :]], 0)
    grad_feats = (
        local_grad + jnp.einsum("sp,sd->pd", send_hot, received, preferred_element_type=F32)
    ).astype(BF16)
    self_sum, edge_sum, head_totals = lax.optimization_barrier((self_sum, edge_sum, head_totals))
    tail_totals = lax.psum((self_sum, edge_sum), ("group", "dom"))
    grad_scale = 1.0 / math.sqrt(pin_count * owners)
    return (
        predicted,
        grad_feats,
        tail_totals[0] * grad_scale,
        tail_totals[1] * grad_scale,
        head_totals[:feat_width] * grad_scale,
        head_totals[feat_width] * grad_scale,
    )


def solution(mesh):
    in_specs = (
        P(("group", "dom"), None),
        P(),
        P(),
        P(),
        P(),
        P(("group", "dom"), None),
        P(("group", "dom"), None, None),
        P(("group", "dom"), None, None),
        P(("group", "dom"), None),
        P(("group", "dom")),
        P(("group", "dom")),
    )
    out_specs = (P(("group", "dom")), P(("group", "dom"), None), P(), P(), P(), P())
    return jax.shard_map(
        on_device, mesh=mesh, in_specs=in_specs, out_specs=out_specs, check_vma=False
    )
```

profile of v0, /device:TPU:0, one launch (start us, length us, event | category | flops | bytes accessed | tf_op | source)
XLA Modules:
  0.0 383.9 jit_solution(4948331850442410509)
XLA Ops:
  7.2 0.7 add_convert_fusion
  7.9 1.3 fusion.31
  9.3 0.7 multiply_add_fusion
  10.0 1.5 fusion.11
  11.5 0.7 sub.16
  12.2 7.3 %all-to-all-start = ((s32[32,1,64]{2,1,0:T(1,128)}), s32[32,1,64]{2,1,0:T(1,128)S(1)}, u32[]{:S(2)}, u32[]{:S(2)}) async-start(s32[32,1,64]{2,1,0:T(1,128)} %sub.16), calls=%async_computation | async-start | bytes 32768 | tf_op jit(solution)/shard_map/all_to_all | solution.py:92
  19.5 0.5 fusion.28
  20.1 2.2 collective-permute-start
  22.2 1.3 collective-permute-start.1
  23.5 1.9 convert_reduce_fusion
  25.5 0.3 fusion.55
  25.8 0.8 collective-permute-done.1
  26.6 4.8 %fusion.20 = bf16[4,1024,256]{2,1,0:T(8,128)(2,1)S(1)} fusion(s32[4,1024]{1,0:T(4,128)S(1)} %bitcast.74, bf16[256,256]{1,0:T(8,128)(2,1)S(1)} %collective-permute-done.1, bf16[256,256]{1,0:T(8,128)(2,1)S(1)} %collective-permute-done, bf16[1024,256]{1,0:T(8,128)(2,1)S(1)} %copy-done.2), kind=kOutput, calls=%fused_computation.29 | convolution fusion | flops 3230924800 | bytes 2899968 | tf_op jit(solution)/shard_map/ter,rd->ted/dot_general | solution.py:64
  31.5 5.8 %fusion.4 = f32[4,1024,256]{2,1,0:T(8,128)S(1)} fusion(bf16[4,1024,256]{2,1,0:T(8,128)(2,1)S(1)} %fusion.20, s32[4,1024]{1,0:T(4,128)S(1)} %bitcast.72), kind=kOutput, calls=%fused_computation.7 | convolution fusion | flops 2151677952 | bytes 6307840 | tf_op jit(solution)/shard_map/tep,ted->tpd/dot_general | solution.py:67
  37.2 2.1 fusion.24
  39.3 1.0 copy-done.7
  40.3 3.5 fusion.16
  43.8 7.9 %all-to-all-start.1 = ((bf16[32,64,256]{2,1,0:T(8,128)(2,1)}), bf16[32,64,256]{2,1,0:T(8,128)(2,1)}, u32[]{:S(2)}, u32[]{:S(2)}) async-start(bf16[32,64,256]{2,1,0:T(8,128)(2,1)} %bitcast.60), calls=%async_computation.1 | async-start | bytes 2097152 | tf_op jit(solution)/shard_map/all_to_all | solution.py:100
  51.8 0.5 broadcast.42
  52.3 0.7 reduce.3
  53.0 26.2 %all-to-all-done.1 = bf16[32,64,256]{2,1,0:T(8,128)(2,1)} async-done(((bf16[32,64,256]{2,1,0:T(8,128)(2,1)}), bf16[32,64,256]{2,1,0:T(8,128)(2,1)}, u32[]{:S(2)}, u32[]{:S(2)}) %all-to-all-start.1) | async-done | bytes 1048608 | tf_op jit(solution)/shard_map/all_to_all | solution.py:100
  79.3 2.3 fusion.29
  81.6 0.4 multiply_convert_fusion.2
  82.1 0.8 copy-done.4
  83.1 1.2 multiply_convert_fusion.1
  84.3 3.0 convolution_convert_fusion
  87.3 3.4 all-to-all-start.2
  90.8 1.4 fusion.59
  92.1 1.4 fusion.58
  93.5 1.2 pad_maximum_fusion
  94.8 26.5 %all-to-all-done.2 = bf16[32,64,256]{2,1,0:T(8,128)(2,1)} async-done(((bf16[32,64,256]{2,1,0:T(8,128)(2,1)}), bf16[32,64,256]{2,1,0:T(8,128)(2,1)}, u32[]{:S(2)}, u32[]{:S(2)}) %all-to-all-start.2) | async-done | bytes 1048608 | tf_op jit(solution)/shard_map/all_to_all | solution.py:120
  121.2 3.3 fusion.26
  124.6 3.3 fusion.21
  127.9 9.3 %fusion = f32[4,1536,256]{2,1,0:T(8,128)} fusion(bf16[4,1024,256]{2,1,0:T(8,128)(2,1)S(1)} %fusion.21, s32[4,1024]{1,0:T(4,128)S(1)} %bitcast.75), kind=kOutput, calls=%fused_computation.1 | convolution fusion | flops 3227516928 | bytes 8404992 | tf_op jit(solution)/shard_map/ter,ted->trd/dot_general | solution.py:135
  137.2 1.0 convolution_bitcast_fusion.2
  138.3 1.9 fusion.57
  140.2 89.8 %all-reduce.4.cloned.1.call-done = f32[257,1024]{1,0:T(8,128)} async-done(((f32[257,1024]{1,0:T(8,128)}), f32[257,1024]{1,0:T(8,128)}) %all-reduce.4.cloned.1.call-update) | async-done | bytes 1052688 | tf_op jit(solution)/shard_map/psum | solution.py:117
  229.9 5.1 %fusion.54 = (bf16[1536,256]{1,0:T(8,128)(2,1)S(1)}, f32[1536,256]{1,0:T(8,128)S(1)}) fusion(f32[4,1536,256]{2,1,0:T(8,128)} %fusion, bf16[4,256,256]{2,1,0:T(8,128)(2,1)S(1)} %copy-done.1), kind=kOutput, calls=%fused_computation.83 | convolution fusion | flops 4832231424 | bytes 9175040 | tf_op jit(solution)/shard_map/trd,tkd->rk/dot_general | solution.py:34
  235.1 2.1 collective-permute-start.2
  237.2 1.3 collective-permute-start.3
  238.5 0.3 convolution_add_fusion
  238.9 2.3 slice_multiply_fusion
  241.2 1.4 slice_multiply_fusion.1
  242.6 1.6 fusion.27
  244.2 128.8 %all-reduce.6.cloned.1.call-done = (f32[256,256]{0,1:T(8,128)}, f32[4,256,256]{2,1,0:T(8,128)}) async-done(((f32[256,256]{0,1:T(8,128)}, f32[4,256,256]{2,1,0:T(8,128)}), (f32[256,256]{0,1:T(8,128)}, f32[4,256,256]{2,1,0:T(8,128)})) %all-reduce.6.cloned.1.call-update) | async-done | bytes 1310736 | tf_op jit(solution)/shard_map/psum | solution.py:148
  373.0 1.0 broadcast_multiply_fusion.1
  373.9 0.8 copy.18
  374.8 2.3 broadcast_multiply_fusion
  (47 shorter events, 0.6 us)
Async XLA Ops:
  7.2 74.4 %copy-start = (bf16[256,1024]{1,0:T(8,128)(2,1)S(1)}, bf16[256,1024]{1,0:T(8,128)(2,1)}, u32[]{:S(2)}) copy-start(bf16[256,1024]{1,0:T(8,128)(2,1)} %param.14) | copy-start | bytes 1572868
  9.2 10.3 %copy-start.2 = (bf16[1024,256]{1,0:T(8,128)(2,1)S(1)}, bf16[1024,256]{1,0:T(8,128)(2,1)}, u32[]{:S(2)}) copy-start(bf16[1024,256]{1,0:T(8,128)(2,1)} %param.11) | copy-start | bytes 1572868
  9.3 10.3 %copy-start.14 = (s32[1,512]{1,0:T(1,128)S(1)}, s32[1,512]{1,0:T(1,128)}, u32[]{:S(2)}) copy-start(s32[1,512]{1,0:T(1,128)} %param.16) | copy-start | bytes 6148
  10.0 13.5 %copy-start.12 = (s32[1,4,1024]{2,1,0:T(4,128)S(1)}, s32[1,4,1024]{2,1,0:T(4,128)}, u32[]{:S(2)}) copy-start(s32[1,4,1024]{2,1,0:T(4,128)} %param.18) | copy-start | bytes 49156
  10.0 15.5 %copy-start.8 = (bf16[256,256]{1,0:T(8,128)(2,1)S(1)}, bf16[256,256]{1,0:T(8,128)(2,1)}, u32[]{:S(2)}) copy-start(bf16[256,256]{1,0:T(8,128)(2,1)} %param.12) | copy-start | bytes 393220
  11.5 15.1 %copy-start.13 = (s32[1,4,1024]{2,1,0:T(4,128)S(1)}, s32[1,4,1024]{2,1,0:T(4,128)}, u32[]{:S(2)}) copy-start(s32[1,4,1024]{2,1,0:T(4,128)} %param.17) | copy-start | bytes 49156
  12.2 31.6 %all-to-all-start = ((s32[32,1,64]{2,1,0:T(1,128)}), s32[32,1,64]{2,1,0:T(1,128)S(1)}, u32[]{:S(2)}, u32[]{:S(2)}) async-start(s32[32,1,64]{2,1,0:T(1,128)} %sub.16), calls=%async_computation | async-start | bytes 32768 | tf_op jit(solution)/shard_map/all_to_all | solution.py:92
  20.1 5.8 %collective-permute-start = (bf16[256,256]{1,0:T(8,128)(2,1)S(1)}, bf16[256,256]{1,0:T(8,128)(2,1)S(1)}, u32[]{:S(2)}, u32[]{:S(2)}) collective-permute-start(bf16[256,256]{1,0:T(8,128)(2,1)S(1)} %get-tuple-element.22), channel_id=1, source_target_pairs={{0,1},{1,2},{2,3},{3,4},{4,5},{5,6},{6,7},{8,9},{9,10},{10,11},{11... | collective-permute-start | bytes 393224 | tf_op jit(solution)/shard_map/ppermute | solution.py:16
  22.2 4.4 %collective-permute-start.1 = (bf16[256,256]{1,0:T(8,128)(2,1)S(1)}, bf16[256,256]{1,0:T(8,128)(2,1)S(1)}, u32[]{:S(2)}, u32[]{:S(2)}) collective-permute-start(bf16[256,256]{1,0:T(8,128)(2,1)S(1)} %get-tuple-element.23), channel_id=1, source_target_pairs={{1,0},{2,1},{3,2},{4,3},{5,4},{6,5},{7,6},{9,8},{10,9},{11,10},{12... | collective-permute-start | bytes 393224 | tf_op jit(solution)/shard_map/ppermute | solution.py:19
  31.5 5.8 %copy-start.1 = (bf16[4,256,256]{2,1,0:T(8,128)(2,1)S(1)}, bf16[4,256,256]{2,1,0:T(8,128)(2,1)}, u32[]{:S(2)}) copy-start(bf16[4,256,256]{2,1,0:T(8,128)(2,1)} %param.13) | copy-start | bytes 1572868
  39.3 1.0 copy-start.7
  43.8 7.9 %copy-start.9 = (bf16[1024]{0:T(1024)(128)(2,1)S(1)}, bf16[1024]{0:T(1024)(128)(2,1)}, u32[]{:S(2)}) copy-start(bf16[1024]{0:T(1024)(128)(2,1)} %param.15) | copy-start | bytes 6148
  43.8 35.5 %all-to-all-start.1 = ((bf16[32,64,256]{2,1,0:T(8,128)(2,1)}), bf16[32,64,256]{2,1,0:T(8,128)(2,1)}, u32[]{:S(2)}, u32[]{:S(2)}) async-start(bf16[32,64,256]{2,1,0:T(8,128)(2,1)} %bitcast.60), calls=%async_computation.1 | async-start | bytes 2097152 | tf_op jit(solution)/shard_map/all_to_all | solution.py:100
  81.6 1.5 copy-start.11
  82.0 0.8 copy-start.4
  83.1 4.2 %copy-start.10 = (f32[1,256]{1,0:T(1,128)}, f32[1,256]{1,0:T(1,128)S(1)}, u32[]{:S(2)}) copy-start(f32[1,256]{1,0:T(1,128)S(1)} %fusion.56) | copy-start | bytes 3076
  87.3 33.9 %all-to-all-start.2 = ((bf16[32,64,256]{2,1,0:T(8,128)(2,1)}), bf16[32,64,256]{2,1,0:T(8,128)(2,1)}, u32[]{:S(2)}, u32[]{:S(2)}) async-start(bf16[32,64,256]{2,1,0:T(8,128)(2,1)} %bitcast.59), calls=%async_computation.2 | async-start | bytes 2097152 | tf_op jit(solution)/shard_map/all_to_all | solution.py:120
  90.7 139.2 %all-reduce.4.cloned.1.call-start = ((), (), s32[]{:S(2)}) async-start(), calls=%async_computation.3 | async-start | bytes 2162688 | tf_op jit(solution)/shard_map/psum | solution.py:117
  94.7 278.2 %all-reduce.6.cloned.1.call-start = ((), (), s32[]{:S(2)}) async-start(), calls=%async_computation.4 | async-start | bytes 2621440 | tf_op jit(solution)/shard_map/psum | solution.py:148
  124.6 12.7 %copy-start.5 = (bf16[1024,256]{1,0:T(8,128)(2,1)}, bf16[1024,256]{1,0:T(8,128)(2,1)S(1)}, u32[]{:S(2)}) copy-start(bf16[1024,256]{1,0:T(8,128)(2,1)S(1)} %fusion.26) | copy-start | bytes 1572868
  127.9 9.4 %copy-start.3 = (bf16[1024,256]{1,0:T(8,128)(2,1)S(1)}, bf16[1024,256]{1,0:T(8,128)(2,1)}, u32[]{:S(2)}) copy-start(bf16[1024,256]{1,0:T(8,128)(2,1)} %param.11) | copy-start | bytes 1572868
  140.2 98.3 %copy-start.6 = (bf16[1024,256]{1,0:T(8,128)(2,1)S(1)}, bf16[1024,256]{1,0:T(8,128)(2,1)}, u32[]{:S(2)}) copy-start(bf16[1024,256]{1,0:T(8,128)(2,1)} %copy-done.5) | copy-start | bytes 1572868
  235.1 7.5 %collective-permute-start.2 = (bf16[256,256]{1,0:T(8,128)(2,1)S(1)}, bf16[256,256]{1,0:T(8,128)(2,1)S(1)}, u32[]{:S(2)}, u32[]{:S(2)}) collective-permute-start(bf16[256,256]{1,0:T(8,128)(2,1)S(1)} %get-tuple-element.20), channel_id=1, source_target_pairs={{0,1},{1,2},{2,3},{3,4},{4,5},{5,6},{6,7},{8,9},{9,10},{10,11},{11... | collective-permute-start | bytes 393224 | tf_op jit(solution)/shard_map/ppermute | solution.py:16
  237.2 5.4 %collective-permute-start.3 = (bf16[256,256]{1,0:T(8,128)(2,1)S(1)}, bf16[256,256]{1,0:T(8,128)(2,1)S(1)}, u32[]{:S(2)}, u32[]{:S(2)}) collective-permute-start(bf16[256,256]{1,0:T(8,128)(2,1)S(1)} %get-tuple-element.21), channel_id=1, source_target_pairs={{1,0},{2,1},{3,2},{4,3},{5,4},{6,5},{7,6},{9,8},{10,9},{11,10},{12... | collective-permute-start | bytes 393224 | tf_op jit(solution)/shard_map/ppermute | solution.py:19
Sparse Core Ops, SparseCore 0:
  97.0 132.9 all-reduce.3
  239.0 133.9 all-reduce.5
where the time goes:
time: 385 us; the launch traced here: 384 us
  waiting for transfers between devices  272 us (71%)
  matrix products  54.4 us (14%)
  starting transfers between devices  25.5 us (7%)
  between operations  14.4 us (4%)
  other arithmetic  13.6 us (4%)
  local copies, waits for them, and re-layouts  3.99 us (1%)
    psum x1, waiting for transfers between devices, on_device(): tail_totals = lax.psum((self_sum, edge_sum), ('group', 'dom'))  129 us
    psum x1, waiting for transfers between devices, on_device(): lax.psum(jnp.concatenate([head_sum, out_sum[None, :]], 0), ('group', 'dom'))  89.8 us
    all_to_all x1, waiting for transfers between devices, on_device(): lax.all_to_all(returned.reshape(owners, capacity, feat_width), ('group',...  26.5 us
    all_to_all x1, waiting for transfers between devices, on_device(): lax.all_to_all(outbound.reshape(owners, capacity, feat_width), ('group',...  26.2 us
    dot_general x1, matrix products, on_device(): jnp.einsum('ter,ted->trd', src_hot, edge_rows, preferred_element_type=F32)  9.33 us
    all_to_all x1, starting transfers between devices, on_device(): lax.all_to_all(outbound.reshape(owners, capacity, feat_width), ('group',...  7.91 us
  transfers between devices with their start and end apart: 9, of which 5 were waited for; matrix products, arithmetic and copies ran while one was open for 13% of the time, Pallas kernels for 0%

commit v1 on v0

--- a/solution.py
+++ b/solution.py
@@ -145,7 +145,7 @@
         local_grad + jnp.einsum("sp,sd->pd", send_hot, received, preferred_element_type=F32)
     ).astype(BF16)
     self_sum, edge_sum, head_totals = lax.optimization_barrier((self_sum, edge_sum, head_totals))
-    tail_totals = lax.psum((self_sum, edge_sum), ("group", "dom"))
+    tail_totals = lax.psum(lax.psum((self_sum, edge_sum), "dom"), "group")
     grad_scale = 1.0 / math.sqrt(pin_count * owners)
     return (
         predicted,

time: 385 us -> 364 us (0.945)
  waiting for transfers between devices: 272 us -> 253 us
    psum x1 -> x2, waiting for transfers between devices: 129 us -> 99.6 us  [on_device(): tail_totals = lax.psum(lax.psum((self_sum, edge_sum), 'dom'), 'group')]
    psum x1, waiting for transfers between devices: 89.8 us -> 98.7 us  [on_device(): lax.psum(jnp.concatenate([head_sum, out_sum[None, :]], 0), ('group', 'dom'))]
  transfers between devices with their start and end apart: 9 -> 10, of which waited for: 5 -> 7; matrix products, arithmetic and copies ran while one was open for 13% -> 15% of each run, Pallas kernels for 0% -> 0%
where the time goes in v1:
time: 364 us; the launch traced here: 363 us
  waiting for transfers between devices  253 us (70%)
  matrix products  55.9 us (15%)
  starting transfers between devices  25.1 us (7%)
  between operations  14.2 us (4%)
  other arithmetic  11.5 us (3%)
  local copies, waits for them, and re-layouts  4.13 us (1%)
    psum x2, waiting for transfers between devices, on_device(): tail_totals = lax.psum(lax.psum((self_sum, edge_sum), 'dom'), 'group')  99.6 us
    psum x1, waiting for transfers between devices, on_device(): lax.psum(jnp.concatenate([head_sum, out_sum[None, :]], 0), ('group', 'dom'))  98.7 us
    all_to_all x1, waiting for transfers between devices, on_device(): lax.all_to_all(returned.reshape(owners, capacity, feat_width), ('group',...  26.6 us
    all_to_all x1, waiting for transfers between devices, on_device(): lax.all_to_all(outbound.reshape(owners, capacity, feat_width), ('group',...  26.2 us
    dot_general x1, matrix products, on_device(): jnp.einsum('ter,ted->trd', src_hot, edge_rows, preferred_element_type=F32)  10.5 us
    all_to_all x1, starting transfers between devices, on_device(): lax.all_to_all(outbound.reshape(owners, capacity, feat_width), ('group',...  7.91 us
    all_to_all x1, starting transfers between devices, on_device(): lax.all_to_all(slot_nets.reshape(owners, capacity), ('group', 'dom'), spl...  7.3 us
    dot_general x2, matrix products, split_dot(): jnp.einsum(spec, left, right.astype(F32), precision=lax.Precision.HIGHEST...  7.29 us
  transfers between devices with their start and end apart: 10, of which 7 were waited for; matrix products, arithmetic and copies ran while one was open for 15% of the time, Pallas kernels for 0%

profile of v1, /device:TPU:0, one launch (start us, length us, event | category | flops | bytes accessed | tf_op | source)
XLA Modules:
  0.0 363.2 jit_solution(11657426355957896693)
XLA Ops:
  7.2 0.7 add_convert_fusion
  7.9 1.3 fusion.31
  9.3 0.7 multiply_add_fusion
  10.0 1.5 fusion.11
  11.5 0.7 sub.16
  12.2 7.3 %all-to-all-start = ((s32[32,1,64]{2,1,0:T(1,128)}), s32[32,1,64]{2,1,0:T(1,128)S(1)}, u32[]{:S(2)}, u32[]{:S(2)}) async-start(s32[32,1,64]{2,1,0:T(1,128)} %sub.16), calls=%async_computation | async-start | bytes 32768 | tf_op jit(solution)/shard_map/all_to_all | solution.py:92
  19.5 0.5 fusion.28
  20.1 2.2 collective-permute-start
  22.2 1.3 collective-permute-start.1
  23.5 1.9 convert_reduce_fusion
  25.8 0.8 collective-permute-done.1
  26.6 4.8 %fusion.20 = bf16[4,1024,256]{2,1,0:T(8,128)(2,1)S(1)} fusion(s32[4,1024]{1,0:T(4,128)S(1)} %bitcast.74, bf16[256,256]{1,0:T(8,128)(2,1)S(1)} %collective-permute-done.1, bf16[256,256]{1,0:T(8,128)(2,1)S(1)} %collective-permute-done, bf16[1024,256]{1,0:T(8,128)(2,1)S(1)} %copy-done.3), kind=kOutput, calls=%fused_computation.29 | convolution fusion | flops 3230924800 | bytes 2899968 | tf_op jit(solution)/shard_map/ter,rd->ted/dot_general | solution.py:64
  31.5 5.8 %fusion.4 = f32[4,1024,256]{2,1,0:T(8,128)S(1)} fusion(bf16[4,1024,256]{2,1,0:T(8,128)(2,1)S(1)} %fusion.20, s32[4,1024]{1,0:T(4,128)S(1)} %bitcast.72), kind=kOutput, calls=%fused_computation.7 | convolution fusion | flops 2151677952 | bytes 6307840 | tf_op jit(solution)/shard_map/tep,ted->tpd/dot_general | solution.py:67
  37.2 2.1 fusion.24
  39.3 1.0 copy-done.8
  40.3 3.5 fusion.16
  43.8 7.9 %all-to-all-start.1 = ((bf16[32,64,256]{2,1,0:T(8,128)(2,1)}), bf16[32,64,256]{2,1,0:T(8,128)(2,1)}, u32[]{:S(2)}, u32[]{:S(2)}) async-start(bf16[32,64,256]{2,1,0:T(8,128)(2,1)} %bitcast.60), calls=%async_computation.1 | async-start | bytes 2097152 | tf_op jit(solution)/shard_map/all_to_all | solution.py:100
  51.8 0.5 broadcast.42
  52.3 0.7 reduce.3
  53.0 26.2 %all-to-all-done.1 = bf16[32,64,256]{2,1,0:T(8,128)(2,1)} async-done(((bf16[32,64,256]{2,1,0:T(8,128)(2,1)}), bf16[32,64,256]{2,1,0:T(8,128)(2,1)}, u32[]{:S(2)}, u32[]{:S(2)}) %all-to-all-start.1) | async-done | bytes 1048608 | tf_op jit(solution)/shard_map/all_to_all | solution.py:100
  79.3 2.3 fusion.29
  81.6 0.4 multiply_convert_fusion.2
  82.1 0.8 copy-done.5
  83.1 1.2 multiply_convert_fusion.1
  84.3 3.0 convolution_convert_fusion
  87.3 3.4 all-to-all-start.2
  90.8 1.4 fusion.59
  92.1 1.4 fusion.58
  93.5 1.1 pad_maximum_fusion
  94.7 26.6 %all-to-all-done.2 = bf16[32,64,256]{2,1,0:T(8,128)(2,1)} async-done(((bf16[32,64,256]{2,1,0:T(8,128)(2,1)}), bf16[32,64,256]{2,1,0:T(8,128)(2,1)}, u32[]{:S(2)}, u32[]{:S(2)}) %all-to-all-start.2) | async-done | bytes 1048608 | tf_op jit(solution)/shard_map/all_to_all | solution.py:120
  121.3 3.3 fusion.26
  124.6 3.3 fusion.21
  127.9 1.3 convolution_bitcast_fusion.2
  129.4 1.9 fusion.57
  131.2 98.7 %all-reduce.6.cloned.1.call-done = f32[257,1024]{1,0:T(8,128)} async-done(((f32[257,1024]{1,0:T(8,128)}), f32[257,1024]{1,0:T(8,128)}) %all-reduce.6.cloned.1.call-update) | async-done | bytes 1052688 | tf_op jit(solution)/shard_map/psum | solution.py:117
  230.2 10.5 %fusion = f32[4,1536,256]{2,1,0:T(8,128)} fusion(bf16[4,1024,256]{2,1,0:T(8,128)(2,1)} %copy-done.2, s32[4,1024]{1,0:T(4,128)S(1)} %bitcast.75), kind=kOutput, calls=%fused_computation.1 | convolution fusion | flops 3227516928 | bytes 8404992 | tf_op jit(solution)/shard_map/ter,ted->trd/dot_general | solution.py:135
  240.7 52.8 %all-reduce.8.cloned.1.call-done = (f32[256,256]{0,1:T(8,128)}, f32[4,256,256]{2,1,0:T(8,128)}) async-done(((f32[256,256]{0,1:T(8,128)}, f32[4,256,256]{2,1,0:T(8,128)}), (f32[256,256]{0,1:T(8,128)}, f32[4,256,256]{2,1,0:T(8,128)})) %all-reduce.8.cloned.1.call-update) | async-done | bytes 1310736 | tf_op jit(solution)/shard_map/psum | solution.py:148
  293.5 5.2 %fusion.54 = (bf16[1536,256]{1,0:T(8,128)(2,1)S(1)}, f32[1536,256]{1,0:T(8,128)S(1)}) fusion(f32[4,1536,256]{2,1,0:T(8,128)} %fusion, bf16[4,256,256]{2,1,0:T(8,128)(2,1)S(1)} %copy-done.1), kind=kOutput, calls=%fused_computation.83 | convolution fusion | flops 4832231424 | bytes 9175040 | tf_op jit(solution)/shard_map/trd,tkd->rk/dot_general | solution.py:34
  298.8 1.4 collective-permute-start.2
  300.2 1.3 collective-permute-start.3
  301.5 1.1 slice_multiply_fusion
  303.0 0.6 slice_multiply_fusion.1
  303.6 0.6 collective-permute-done.3
  304.1 1.6 fusion.27
  305.8 46.8 %all-reduce.10.cloned.1.call-done = (f32[256,256]{0,1:T(8,128)}, f32[4,256,256]{2,1,0:T(8,128)}) async-done(((f32[256,256]{0,1:T(8,128)}, f32[4,256,256]{2,1,0:T(8,128)}), (f32[256,256]{0,1:T(8,128)}, f32[4,256,256]{2,1,0:T(8,128)})) %all-reduce.10.cloned.1.call-update) | async-done | bytes 1310736 | tf_op jit(solution)/shard_map/psum | solution.py:148
  352.6 1.0 broadcast_multiply_fusion.1
  353.6 0.8 copy.18
  354.4 2.3 broadcast_multiply_fusion
  (54 shorter events, 1.6 us)
Async XLA Ops:
  7.2 74.4 %copy-start = (bf16[256,1024]{1,0:T(8,128)(2,1)S(1)}, bf16[256,1024]{1,0:T(8,128)(2,1)}, u32[]{:S(2)}) copy-start(bf16[256,1024]{1,0:T(8,128)(2,1)} %param.14) | copy-start | bytes 1572868
  9.2 10.3 %copy-start.3 = (bf16[1024,256]{1,0:T(8,128)(2,1)S(1)}, bf16[1024,256]{1,0:T(8,128)(2,1)}, u32[]{:S(2)}) copy-start(bf16[1024,256]{1,0:T(8,128)(2,1)} %param.11) | copy-start | bytes 1572868
  9.3 10.3 %copy-start.16 = (s32[1,512]{1,0:T(1,128)S(1)}, s32[1,512]{1,0:T(1,128)}, u32[]{:S(2)}) copy-start(s32[1,512]{1,0:T(1,128)} %param.16) | copy-start | bytes 6148
  10.0 13.5 %copy-start.14 = (s32[1,4,1024]{2,1,0:T(4,128)S(1)}, s32[1,4,1024]{2,1,0:T(4,128)}, u32[]{:S(2)}) copy-start(s32[1,4,1024]{2,1,0:T(4,128)} %param.18) | copy-start | bytes 49156
  10.0 15.5 %copy-start.10 = (bf16[256,256]{1,0:T(8,128)(2,1)S(1)}, bf16[256,256]{1,0:T(8,128)(2,1)}, u32[]{:S(2)}) copy-start(bf16[256,256]{1,0:T(8,128)(2,1)} %param.12) | copy-start | bytes 393220
  11.5 15.1 %copy-start.15 = (s32[1,4,1024]{2,1,0:T(4,128)S(1)}, s32[1,4,1024]{2,1,0:T(4,128)}, u32[]{:S(2)}) copy-start(s32[1,4,1024]{2,1,0:T(4,128)} %param.17) | copy-start | bytes 49156
  12.2 31.6 %all-to-all-start = ((s32[32,1,64]{2,1,0:T(1,128)}), s32[32,1,64]{2,1,0:T(1,128)S(1)}, u32[]{:S(2)}, u32[]{:S(2)}) async-start(s32[32,1,64]{2,1,0:T(1,128)} %sub.16), calls=%async_computation | async-start | bytes 32768 | tf_op jit(solution)/shard_map/all_to_all | solution.py:92
  20.1 5.8 %collective-permute-start = (bf16[256,256]{1,0:T(8,128)(2,1)S(1)}, bf16[256,256]{1,0:T(8,128)(2,1)S(1)}, u32[]{:S(2)}, u32[]{:S(2)}) collective-permute-start(bf16[256,256]{1,0:T(8,128)(2,1)S(1)} %get-tuple-element.24), channel_id=1, source_target_pairs={{0,1},{1,2},{2,3},{3,4},{4,5},{5,6},{6,7},{8,9},{9,10},{10,11},{11... | collective-permute-start | bytes 393224 | tf_op jit(solution)/shard_map/ppermute | solution.py:16
  22.2 4.4 %collective-permute-start.1 = (bf16[256,256]{1,0:T(8,128)(2,1)S(1)}, bf16[256,256]{1,0:T(8,128)(2,1)S(1)}, u32[]{:S(2)}, u32[]{:S(2)}) collective-permute-start(bf16[256,256]{1,0:T(8,128)(2,1)S(1)} %get-tuple-element.25), channel_id=1, source_target_pairs={{1,0},{2,1},{3,2},{4,3},{5,4},{6,5},{7,6},{9,8},{10,9},{11,10},{12... | collective-permute-start | bytes 393224 | tf_op jit(solution)/shard_map/ppermute | solution.py:19
  31.5 5.8 %copy-start.1 = (bf16[4,256,256]{2,1,0:T(8,128)(2,1)S(1)}, bf16[4,256,256]{2,1,0:T(8,128)(2,1)}, u32[]{:S(2)}) copy-start(bf16[4,256,256]{2,1,0:T(8,128)(2,1)} %param.13) | copy-start | bytes 1572868
  39.3 1.0 copy-start.8
  43.8 7.9 %copy-start.11 = (bf16[1024]{0:T(1024)(128)(2,1)S(1)}, bf16[1024]{0:T(1024)(128)(2,1)}, u32[]{:S(2)}) copy-start(bf16[1024]{0:T(1024)(128)(2,1)} %param.15) | copy-start | bytes 6148
  43.8 35.5 %all-to-all-start.1 = ((bf16[32,64,256]{2,1,0:T(8,128)(2,1)}), bf16[32,64,256]{2,1,0:T(8,128)(2,1)}, u32[]{:S(2)}, u32[]{:S(2)}) async-start(bf16[32,64,256]{2,1,0:T(8,128)(2,1)} %bitcast.60), calls=%async_computation.1 | async-start | bytes 2097152 | tf_op jit(solution)/shard_map/all_to_all | solution.py:100
  81.6 1.5 copy-start.13
  82.0 0.8 copy-start.5
  83.1 4.2 %copy-start.12 = (f32[1,256]{1,0:T(1,128)}, f32[1,256]{1,0:T(1,128)S(1)}, u32[]{:S(2)}) copy-start(f32[1,256]{1,0:T(1,128)S(1)} %fusion.56) | copy-start | bytes 3076
  87.3 33.9 %all-to-all-start.2 = ((bf16[32,64,256]{2,1,0:T(8,128)(2,1)}), bf16[32,64,256]{2,1,0:T(8,128)(2,1)}, u32[]{:S(2)}, u32[]{:S(2)}) async-start(bf16[32,64,256]{2,1,0:T(8,128)(2,1)} %bitcast.59), calls=%async_computation.2 | async-start | bytes 2097152 | tf_op jit(solution)/shard_map/all_to_all | solution.py:120
  90.7 139.2 %all-reduce.6.cloned.1.call-start = ((), (), s32[]{:S(2)}) async-start(), calls=%async_computation.3 | async-start | bytes 2162688 | tf_op jit(solution)/shard_map/psum | solution.py:117
  94.7 198.9 %all-reduce.8.cloned.1.call-start = ((), (), s32[]{:S(2)}) async-start(), calls=%async_computation.4 | async-start | bytes 2621440 | tf_op jit(solution)/shard_map/psum | solution.py:148
  124.6 3.3 copy-start.6
  124.6 3.3 copy-start.4
  127.9 1.5 copy-start.2
  230.0 122.6 %all-reduce.10.cloned.1.call-start = ((), (), s32[]{:S(2)}) async-start(), calls=%async_computation.5 | async-start | bytes 2621440 | tf_op jit(solution)/shard_map/psum | solution.py:148
  293.5 8.0 %copy-start.9 = (f32[257,1024]{1,0:T(8,128)S(1)}, f32[257,1024]{1,0:T(8,128)}, u32[]{:S(2)}) copy-start(f32[257,1024]{1,0:T(8,128)} %all-reduce.6.cloned.1.call-done) | copy-start | bytes 3158020
  298.8 3.9 %copy-start.7 = (bf16[1024,256]{1,0:T(8,128)(2,1)S(1)}, bf16[1024,256]{1,0:T(8,128)(2,1)}, u32[]{:S(2)}) copy-start(bf16[1024,256]{1,0:T(8,128)(2,1)} %copy-done.6) | copy-start | bytes 1572868
  298.8 4.8 %collective-permute-start.2 = (bf16[256,256]{1,0:T(8,128)(2,1)S(1)}, bf16[256,256]{1,0:T(8,128)(2,1)S(1)}, u32[]{:S(2)}, u32[]{:S(2)}) collective-permute-start(bf16[256,256]{1,0:T(8,128)(2,1)S(1)} %get-tuple-element.22), channel_id=1, source_target_pairs={{0,1},{1,2},{2,3},{3,4},{4,5},{5,6},{6,7},{8,9},{9,10},{10,11},{11... | collective-permute-start | bytes 393224 | tf_op jit(solution)/shard_map/ppermute | solution.py:16
  300.2 3.9 %collective-permute-start.3 = (bf16[256,256]{1,0:T(8,128)(2,1)S(1)}, bf16[256,256]{1,0:T(8,128)(2,1)S(1)}, u32[]{:S(2)}, u32[]{:S(2)}) collective-permute-start(bf16[256,256]{1,0:T(8,128)(2,1)S(1)} %get-tuple-element.23), channel_id=1, source_target_pairs={{1,0},{2,1},{3,2},{4,3},{5,4},{6,5},{7,6},{9,8},{10,9},{11,10},{12... | collective-permute-start | bytes 393224 | tf_op jit(solution)/shard_map/ppermute | solution.py:19
Sparse Core Ops, SparseCore 0:
  97.0 132.9 all-reduce.5
  233.1 60.3 all-reduce.7
  296.9 55.6 all-reduce.9
